TPU v7x, 256 devices: a whole 4x4x8 slice. The times are simulated.
256 devices in a mesh: req: 128 (over x, y, z), tp: 2 (over core).
Axes of the slice: x: 4, y: 4, z: 8, core: 2. Of those that a mesh axis runs over, the one named last changes fastest.
Arguments:
- tokens: bfloat16 [65536, 1024], P('req'), may hold values from -6 to 6
- group_len: int32 [128], P('req'), may hold values from 1 to 512, 49152 in all
- cache_len: int32 [128], replicated, may hold values from 1 to 1024, 65536 in all
- cache_keys: bfloat16 [128, 1024, 1024], P('req', None, 'tp'), may hold values from -192 to 192
- cache_values: bfloat16 [128, 1024, 1024], P('req', None, 'tp'), may hold values from -6 to 6
- w_query: bfloat16 [1024, 1024], P(None, 'tp'), may hold values from -0.1875 to 0.1875
- w_key: bfloat16 [1024, 1024], P(None, 'tp'), may hold values from -0.1875 to 0.1875
- w_value: bfloat16 [1024, 1024], P(None, 'tp'), may hold values from -0.1875 to 0.1875
- w_out: bfloat16 [1024, 1024], P('tp'), may hold values from -0.1875 to 0.1875
- w_up: bfloat16 [1024, 2048], P(None, 'tp'), may hold values from -0.1875 to 0.1875
- w_down: bfloat16 [2048, 1024], P('tp'), may hold values from -0.125 to 0.125
- ln_gains: float32 [2, 1024], replicated, may hold values from 0.5 to 1.5
- ln_biases: float32 [2, 1024], replicated, may hold values from -3 to 3
- embed: bfloat16 [49152, 1024], P(('req', 'tp')), may hold values from -0.5 to 0.5
Outputs:
- layer_out: bfloat16 [65536, 1024], P('req')
- top_logit: float32 [128], P('req')
- shard_top: float32 [128, 256], P(None, ('req', 'tp'))
Inputs may be any that keep to these rules, and one draw needn't show every extreme that they name: `cache_len`: one request has exactly 1024 cached positions. `group_len`: one request has a full block of 512 valid tokens.
All inputs are finite; a program needn't handle non-finite values.
Results may differ from a plain program's by a relative error of at most 0.015.
Values may be sent and summed in bfloat16 or wider, within the bound.
No kernel may reach another device: no remote copies, remote signals or barrier semaphores. Data moves between devices by JAX's collectives and lax.ppermute only.
A program may use at most 128 MiB of HBM per device.

v0:
```python
import jax
import jax.numpy as jnp
from jax import lax
from jax.sharding import PartitionSpec as P

HD = 64
BLK = 256
start_peak = -1e30


def normalize(rows, gain, bias):
    center = rows - jnp.mean(rows, axis=-1, keepdims=True)
    spread = jnp.mean(center * center, axis=-1, keepdims=True)
    return center * lax.rsqrt(spread + 1e-05) * gain + bias


def attend(soft_state, queries, keys_blk, values_blk, allowed):
    row_peak, row_total, accum = soft_state
    scale = 1.0 / jnp.sqrt(jnp.float32(queries.shape[2]))
    scores = (
        jnp.einsum("qhd,khd->qhk", queries, keys_blk, preferred_element_type=jnp.float32) * scale
    )
    scores = jnp.where(allowed[:, None, :], scores, -jnp.inf)
    new_peak = jnp.maximum(row_peak, jnp.max(scores, axis=-1))
    factor = jnp.exp(row_peak - new_peak)
    raised = jnp.exp(scores - new_peak[..., None])
    new_total = row_total * factor + jnp.sum(raised, axis=-1)
    new_accum = accum * factor[..., None] + jnp.einsum(
        "qhk,khd->qhd", raised.astype(jnp.bfloat16), values_blk, preferred_element_type=jnp.float32
    )
    return (new_peak, new_total, new_accum)


def cache_pass(soft_state, queries, keys_all, values_all, offset, blocks, length):

    def one_block(block_idx, carry):
        keys_blk = lax.dynamic_slice_in_dim(keys_all, block_idx * BLK, BLK, 0)
        values_blk = lax.dynamic_slice_in_dim(values_all, block_idx * BLK, BLK, 0)
        places = offset + block_idx * BLK + jnp.arange(BLK, dtype=jnp.int32)
        return attend(carry, queries, keys_blk, values_blk, (places < length)[None, :])

    return lax.fori_loop(jnp.int32(0), blocks, one_block, soft_state)


def shards(
    tokens,
    group_len,
    cache_len,
    cache_keys,
    cache_values,
    w_query,
    w_key,
    w_value,
    w_out,
    w_up,
    w_down,
    ln_gains,
    ln_biases,
    embed,
):
    block_rows = tokens.shape[0]
    local_width = w_query.shape[1]
    heads_local = local_width // HD
    cache_rows = cache_keys.shape[1]
    my_index = lax.axis_index("req")
    my_cache = lax.dynamic_index_in_dim(cache_len, my_index, 0, keepdims=False)
    my_valid = group_len[0]
    queries = jnp.dot(tokens, w_query, preferred_element_type=jnp.float32).astype(jnp.bfloat16)
    keys_new = jnp.dot(tokens, w_key, preferred_element_type=jnp.float32).astype(jnp.bfloat16)
    values_new = jnp.dot(tokens, w_value, preferred_element_type=jnp.float32).astype(jnp.bfloat16)
    head_queries = queries.reshape(block_rows, heads_local, HD)
    empty_state = (
        jnp.full((block_rows, heads_local), start_peak, jnp.float32),
        jnp.zeros((block_rows, heads_local), jnp.float32),
        jnp.zeros((block_rows, heads_local, HD), jnp.float32),
    )
    row_ids = jnp.arange(block_rows, dtype=jnp.int32)
    block_allowed = (row_ids[None, :] <= row_ids[:, None]) & (row_ids < my_valid)[None, :]
    soft_state = attend(
        empty_state,
        head_queries,
        keys_new.reshape(block_rows, heads_local, HD),
        values_new.reshape(block_rows, heads_local, HD),
        block_allowed,
    )
    own_keys = cache_keys[0].reshape(cache_rows, heads_local, HD)
    own_values = cache_values[0].reshape(cache_rows, heads_local, HD)
    own_blocks = (my_cache + BLK - 1) // BLK
    soft_state = cache_pass(soft_state, head_queries, own_keys, own_values, 0, own_blocks, my_cache)
    attn_mixed = (
        (soft_state[2] / soft_state[1][..., None])
        .astype(jnp.bfloat16)
        .reshape(block_rows, local_width)
    )
    attn_sum = lax.psum(
        jnp.dot(attn_mixed, w_out, preferred_element_type=jnp.float32).astype(jnp.bfloat16), "tp"
    ).astype(jnp.float32)
    middle = normalize(tokens.astype(jnp.float32) + attn_sum, ln_gains[0], ln_biases[0]).astype(
        jnp.bfloat16
    )
    active = jax.nn.gelu(
        jnp.dot(middle, w_up, preferred_element_type=jnp.float32), approximate=False
    ).astype(jnp.bfloat16)
    ffn_sum = lax.psum(
        jnp.dot(active, w_down, preferred_element_type=jnp.float32).astype(jnp.bfloat16), "tp"
    ).astype(jnp.float32)
    layer_out = normalize(middle.astype(jnp.float32) + ffn_sum, ln_gains[1], ln_biases[1]).astype(
        jnp.bfloat16
    )
    last_row = lax.dynamic_slice_in_dim(layer_out, my_valid - 1, 1, 0)
    logits = jnp.einsum(
        "rd,vd->rv",
        lax.all_gather(last_row, "req", axis=0, tiled=True),
        embed,
        preferred_element_type=jnp.float32,
    )
    slice_best = jnp.max(logits, axis=1)
    best_logit = lax.pmax(slice_best, ("req", "tp"))
    return (layer_out, lax.dynamic_slice_in_dim(best_logit, my_index, 1, 0), slice_best[:, None])


def solution(mesh):
    placed = (
        P("req", None),
        P("req"),
        P(),
        P("req", None, "tp"),
        P("req", None, "tp"),
        P(None, "tp"),
        P(None, "tp"),
        P(None, "tp"),
        P("tp", None),
        P(None, "tp"),
        P("tp", None),
        P(),
        P(),
        P(("req", "tp"), None),
    )
    return jax.shard_map(
        shards,
        mesh=mesh,
        in_specs=placed,
        out_specs=(P("req", None), P("req"), P(None, ("req", "tp"))),
        check_vma=False,
    )
```

profile of v0, /device:TPU:1, one launch (start us, length us, event | category | flops | bytes accessed | tf_op | source)
XLA Modules:
  0.0 564.5 jit_solution(3807487911290846801)
XLA Ops:
  7.2 0.0 all-reduce.3.cloned.1.call-start
  7.2 1.5 dynamic_slice.16
  10.2 0.1 fusion.79
  10.3 2.3 convolution_convert_fusion.4
  12.6 0.8 convolution_convert_fusion.3
  13.4 1.5 fusion.24
  14.9 1.7 fusion.23
  16.7 1.5 copy-done.1
  18.1 1.6 convolution_convert_fusion.2
  19.7 2.4 copy.27
  22.1 1.4 copy.28
  23.4 5.7 %fusion.45 = f32[512,8,64]{0,2,1:T(8,128)S(1)} fusion(bf16[512,8,64]{0,2,1:T(8,128)(2,1)} %bitcast.92, f32[8,512,512]{2,1,0:T(8,128)} %copy-done.1, f32[512,8]{0,1:T(8,128)S(1)} %broadcast_maximum_fusion, pred[512,512]{0,1:T(8,128)(4,1)S(1)} %fusion.79, f32[512,8]{0,1:T(8,128)S(1)} %get-tuple-element.76), kind=kOutput, calls=%fused_computation.62 | convolution fusion | flops 277086208 | bytes 10256384 | tf_op jit(solution)/shard_map/qhk,khd->qhd/dot_general | solution.py:28
  29.2 23.9 %while.14 = (s32[]{:T(128)}, f32[512,8]{0,1:T(8,128)S(1)}, f32[512,8]{0,1:T(8,128)S(1)}, f32[512,8,64]{0,2,1:T(8,128)S(1)}, s32[]{:T(128)}, /*index=5*/s32[]{:T(...) while((s32[]{:T(128)}, f32[512,8]{0,1:T(8,128)S(1)}, ...), condition=%wide.region_5.6_spmd, body=%wide.region_2.5_spmd.sunk | while | flops 280502784 | bytes 15992003 | solution.py:42
  29.2 0.7 add_compare_fusion.2
  29.9 2.1 bitcast_reduce_fusion.2
  32.0 0.9 fusion.143
  33.0 2.1 fusion.144
  35.2 0.7 add_compare_fusion.2
  35.8 2.1 bitcast_reduce_fusion.2
  38.0 0.9 fusion.143
  38.9 2.1 fusion.144
  41.1 0.7 add_compare_fusion.2
  41.8 2.1 bitcast_reduce_fusion.2
  43.9 0.9 fusion.143
  44.8 2.1 fusion.144
  47.0 0.7 add_compare_fusion.2
  47.7 2.1 bitcast_reduce_fusion.2
  49.8 0.9 fusion.143
  50.8 2.1 fusion.144
  53.1 0.1 divide_convert_fusion
  53.3 3.0 convolution_convert_fusion.1
  56.3 0.0 all-reduce.3.cloned.1.call-update
  56.3 0.0 all-reduce.5.cloned.1.call-start
  56.4 34.8 %all-reduce.3.cloned.1.call-done = bf16[512,1024]{1,0:T(8,128)(2,1)} async-done(((bf16[512,1024]{1,0:T(8,128)(2,1)}), bf16[512,1024]{1,0:T(8,128)(2,1)}) %all-reduce.3.cloned.1.call-update) | async-done | bytes 1048592 | tf_op jit(solution)/shard_map/psum | solution.py:95
  91.2 1.7 fusion.39
  93.0 0.5 multiply_reduce_fusion.1
  93.5 0.5 add_convert_fusion.1
  94.0 8.8 %convolution_convert_fusion = bf16[512,1024]{1,0:T(8,128)(2,1)} fusion(bf16[1024,1024]{1,0:T(8,128)(2,1)S(1)} %copy-done, bf16[512,1024]{1,0:T(8,128)(2,1)S(1)} %add_convert_fusion.1, bf16[1024,1024]{1,0:T(8,128)(2,1)} %param.25), kind=kOutput, calls=%fused_computation.59 | convolution fusion | flops 2182086656 | bytes 6291456 | tf_op jit(solution)/shard_map/dot_general | solution.py:105
  102.8 0.0 all-reduce.5.cloned.1.call-update
  102.9 31.7 %all-reduce.5.cloned.1.call-done = bf16[512,1024]{1,0:T(8,128)(2,1)} async-done(((bf16[512,1024]{1,0:T(8,128)(2,1)}), bf16[512,1024]{1,0:T(8,128)(2,1)}) %all-reduce.5.cloned.1.call-update) | async-done | bytes 1048592 | tf_op jit(solution)/shard_map/psum | solution.py:104
  134.6 1.7 fusion.41
  136.2 0.5 multiply_reduce_fusion
  136.7 0.6 add_convert_fusion
  137.3 1.0 copy-done.8
  138.3 292.9 %all-gather = bf16[128,1,1024]{2,1,0:T(2,128)(2,1)S(1)} all-gather(bf16[1,1,1024]{2,1,0:T(2,128)(2,1)S(1)} %dynamic-slice_bitcast_fusion), channel_id=1, replica_groups=mesh['req'=128,'tp'=2] {'req'}, dimensions={0}, use_global_device_ids=true | all-gather | bytes 264192 | tf_op jit(solution)/shard_map/all_gather | solution.py:113
  431.2 0.3 convolution_reduce_fusion
  431.5 125.6 %pmax.7 = f32[128]{0:T(128)S(1)} all-reduce(f32[128]{0:T(128)S(1)} %convolution_reduce_fusion), channel_id=1, replica_groups=mesh['req'=128,'tp'=2] {'req','tp'}, use_global_device_ids=true, to_apply=%region_13.14 | all-reduce | flops 128 | bytes 1024 | tf_op jit(solution)/shard_map/pmax | solution.py:118
  557.1 0.6 dynamic_slice.18
  (52 shorter events, 0.2 us)
Async XLA Ops:
  7.2 86.9 %copy-start = (bf16[1024,1024]{1,0:T(8,128)(2,1)S(1)}, bf16[1024,1024]{1,0:T(8,128)(2,1)}, u32[]{:S(2)}) copy-start(bf16[1024,1024]{1,0:T(8,128)(2,1)} %param.26) | copy-start | bytes 6291460
  7.2 5.4 copy-start.3
  7.2 84.0 %all-reduce.3.cloned.1.call-start = ((), (), s32[]{:S(2)}) async-start(), calls=%async_computation | async-start | bytes 2097152 | tf_op jit(solution)/shard_map/psum | solution.py:95
  9.4 3.2 copy-start.12
  13.4 1.5 copy-start.2
  14.9 3.2 copy-start.1
  14.9 3.2 copy-start.13
  19.7 2.4 copy-start.9
  53.3 3.1 copy-start.10
  53.3 3.1 copy-start.11
  53.3 37.9 %copy-start.4 = (bf16[512,1024]{1,0:T(8,128)(2,1)S(1)}, bf16[512,1024]{1,0:T(8,128)(2,1)}, u32[]{:S(2)}) copy-start(bf16[512,1024]{1,0:T(8,128)(2,1)} %param.16) | copy-start | bytes 3145732
  56.3 78.2 %all-reduce.5.cloned.1.call-start = ((), (), s32[]{:S(2)}) async-start(), calls=%async_computation.1 | async-start | bytes 2097152 | tf_op jit(solution)/shard_map/psum | solution.py:104
  91.2 1.7 copy-start.7
  91.2 2.2 copy-start.5
  134.6 1.7 copy-start.6
  136.7 294.4 %copy-start.14 = (bf16[192,1024]{1,0:T(8,128)(2,1)S(1)}, bf16[192,1024]{1,0:T(8,128)(2,1)}, u32[]{:S(2)}) copy-start(bf16[192,1024]{1,0:T(8,128)(2,1)} %param.29) | copy-start | bytes 1179652
  137.3 1.0 copy-start.8
  431.5 126.2 %copy-start.15 = (f32[128]{0:T(128)}, f32[128]{0:T(128)S(1)}, u32[]{:S(2)}) copy-start(f32[128]{0:T(128)S(1)} %convolution_reduce_fusion) | copy-start | bytes 1540
Sparse Core Ops, SparseCore 0:
  56.5 34.7 all-reduce.2
  103.0 31.5 all-reduce.4
where the time goes:
time: 565 us
  blocking collectives  419 us (74%)
  waiting for transfers between devices  66.5 us (12%)
  matrix products  40.9 us (7%)
  between operations  15.8 us (3%)
  other arithmetic  14 us (2%)
  local copies, waits for them, and re-layouts  8.34 us (1%)
    all_gather x1, blocking collectives, shards(): lax.all_gather(last_row, 'req', axis=0, tiled=True)  293 us
    pmax x1, blocking collectives, shards(): best_logit = lax.pmax(slice_best, ('req', 'tp'))  126 us
    psum x1, waiting for transfers between devices, shards(): lax.psum(jnp.dot(attn_mixed, w_out, preferred_element_type=jnp.float32).a...  34.8 us
    psum x1, waiting for transfers between devices, shards(): lax.psum(jnp.dot(active, w_down, preferred_element_type=jnp.float32).asty...  31.7 us
    dot_general x5, matrix products, attend(): jnp.einsum('qhk,khd->qhd', raised.astype(jnp.bfloat16), values_blk, prefe...  14.3 us
  transfers between devices with their start and end apart: 2, of which 2 were waited for; matrix products, arithmetic and copies ran while one was open for 0% of the time, Pallas kernels for 0%

commit v1 on v0

--- a/solution.py
+++ b/solution.py
@@ -110,7 +110,9 @@
     last_row = lax.dynamic_slice_in_dim(layer_out, my_valid - 1, 1, 0)
     logits = jnp.einsum(
         "rd,vd->rv",
-        lax.all_gather(last_row, "req", axis=0, tiled=True),
+        jnp.concatenate(
+            lax.all_to_all(jnp.stack([last_row] * lax.axis_size("req")), "req", 0, 0), axis=0
+        ),
         embed,
         preferred_element_type=jnp.float32,
     )

time: 565 us -> 250 us (0.44)
  blocking collectives: 419 us -> 100 us
    all_gather x1 -> x0, blocking collectives: 293 us -> none  [shards(): lax.all_gather(last_row, 'req', axis=0, tiled=True)]
    pmax x1, blocking collectives: 126 us -> 72.4 us  [shards(): best_logit = lax.pmax(slice_best, ('req', 'tp'))]
    all_to_all x0 -> x1, blocking collectives: none -> 27.8 us  [shards(): lax.all_to_all(jnp.stack([last_row] * lax.axis_size('req')), 'req', 0, 0)]
where the time goes in v1:
time: 250 us
  blocking collectives  100 us (40%)
  waiting for transfers between devices  66.5 us (27%)
  matrix products  40.9 us (16%)
  other arithmetic  16.1 us (6%)
  between operations  15.8 us (6%)
  local copies, waits for them, and re-layouts  9.55 us (4%)
    pmax x1, blocking collectives, shards(): best_logit = lax.pmax(slice_best, ('req', 'tp'))  72.4 us
    psum x1, waiting for transfers between devices, shards(): lax.psum(jnp.dot(attn_mixed, w_out, preferred_element_type=jnp.float32).a...  34.8 us
    psum x1, waiting for transfers between devices, shards(): lax.psum(jnp.dot(active, w_down, preferred_element_type=jnp.float32).asty...  31.7 us
    all_to_all x1, blocking collectives, shards(): lax.all_to_all(jnp.stack([last_row] * lax.axis_size('req')), 'req', 0, 0)  27.8 us
    dot_general x5, matrix products, attend(): jnp.einsum('qhk,khd->qhd', raised.astype(jnp.bfloat16), values_blk, prefe...  14.3 us
    dot_general x5, matrix products, attend(): jnp.einsum('qhd,khd->qhk', queries, keys_blk, preferred_element_type=jnp....  9.87 us
    dot_general x1, matrix products, shards(): jnp.dot(active, w_down, preferred_element_type=jnp.float32)  8.8 us
    unnamed x36, local copies, waits for them, and re-layouts  6.64 us
  transfers between devices with their start and end apart: 2, of which 2 were waited for; matrix products, arithmetic and copies ran while one was open for 0% of the time, Pallas kernels for 0%

profile of v1, /device:TPU:1, one launch (start us, length us, event | category | flops | bytes accessed | tf_op | source)
XLA Modules:
  0.0 249.7 jit_solution(926007348870213204)
XLA Ops:
  7.2 1.5 dynamic_slice.18
  10.2 0.1 fusion.79
  10.3 2.3 convolution_convert_fusion.4
  12.6 0.8 convolution_convert_fusion.3
  13.4 1.5 fusion.24
  14.9 1.7 fusion.23
  16.7 1.5 copy-done.1
  18.1 1.6 convolution_convert_fusion.2
  19.7 2.4 copy.27
  22.1 1.4 copy.28
  23.4 5.7 %fusion.45 = f32[512,8,64]{0,2,1:T(8,128)S(1)} fusion(bf16[512,8,64]{0,2,1:T(8,128)(2,1)} %bitcast.90, f32[8,512,512]{2,1,0:T(8,128)} %copy-done.1, f32[512,8]{0,1:T(8,128)S(1)} %broadcast_maximum_fusion, pred[512,512]{0,1:T(8,128)(4,1)S(1)} %fusion.79, f32[512,8]{0,1:T(8,128)S(1)} %get-tuple-element.76), kind=kOutput, calls=%fused_computation.62 | convolution fusion | flops 277086208 | bytes 10256384 | tf_op jit(solution)/shard_map/qhk,khd->qhd/dot_general | solution.py:28
  29.2 23.9 %while.14 = (s32[]{:T(128)}, f32[512,8]{0,1:T(8,128)S(1)}, f32[512,8]{0,1:T(8,128)S(1)}, f32[512,8,64]{0,2,1:T(8,128)S(1)}, s32[]{:T(128)}, /*index=5*/s32[]{:T(...) while((s32[]{:T(128)}, f32[512,8]{0,1:T(8,128)S(1)}, ...), condition=%wide.region_5.6_spmd, body=%wide.region_2.5_spmd.sunk | while | flops 280502784 | bytes 15992003 | solution.py:42
  29.2 0.7 add_compare_fusion.2
  29.9 2.1 bitcast_reduce_fusion.2
  32.0 0.9 fusion.143
  33.0 2.1 fusion.144
  35.2 0.7 add_compare_fusion.2
  35.8 2.1 bitcast_reduce_fusion.2
  38.0 0.9 fusion.143
  38.9 2.1 fusion.144
  41.1 0.7 add_compare_fusion.2
  41.8 2.1 bitcast_reduce_fusion.2
  43.9 0.9 fusion.143
  44.8 2.1 fusion.144
  47.0 0.7 add_compare_fusion.2
  47.7 2.1 bitcast_reduce_fusion.2
  49.8 0.9 fusion.143
  50.8 2.1 fusion.144
  53.3 3.0 %convolution_convert_fusion.1 = bf16[512,1024]{1,0:T(8,128)(2,1)} fusion(bf16[512,512]{0,1:T(8,128)(2,1)S(1)} %bitcast.85, bf16[512,1024]{1,0:T(8,128)(2,1)} %param.24), kind=kOutput, calls=%fused_computation.60 | convolution fusion | flops 537395200 | bytes 2621440 | tf_op jit(solution)/shard_map/dot_general | solution.py:96
  56.4 34.8 %all-reduce.3.cloned.1.call-done = bf16[512,1024]{1,0:T(8,128)(2,1)} async-done(((bf16[512,1024]{1,0:T(8,128)(2,1)}), bf16[512,1024]{1,0:T(8,128)(2,1)}) %all-reduce.3.cloned.1.call-update) | async-done | bytes 1048592 | tf_op jit(solution)/shard_map/psum | solution.py:95
  91.2 1.7 fusion.39
  93.0 0.5 multiply_reduce_fusion.1
  93.5 0.5 add_convert_fusion.1
  94.0 8.8 %convolution_convert_fusion = bf16[512,1024]{1,0:T(8,128)(2,1)} fusion(bf16[1024,1024]{1,0:T(8,128)(2,1)S(1)} %copy-done, bf16[512,1024]{1,0:T(8,128)(2,1)S(1)} %add_convert_fusion.1, bf16[1024,1024]{1,0:T(8,128)(2,1)} %param.25), kind=kOutput, calls=%fused_computation.59 | convolution fusion | flops 2182086656 | bytes 6291456 | tf_op jit(solution)/shard_map/dot_general | solution.py:105
  102.9 31.7 %all-reduce.5.cloned.1.call-done = bf16[512,1024]{1,0:T(8,128)(2,1)} async-done(((bf16[512,1024]{1,0:T(8,128)(2,1)}), bf16[512,1024]{1,0:T(8,128)(2,1)}) %all-reduce.5.cloned.1.call-update) | async-done | bytes 1048592 | tf_op jit(solution)/shard_map/psum | solution.py:104
  134.6 1.7 fusion.41
  136.2 0.5 multiply_reduce_fusion
  136.7 0.6 add_convert_fusion
  137.3 1.0 copy-done.8
  138.3 0.3 stack.2
  138.6 0.5 broadcast.121
  139.1 2.1 reduce.2
  141.3 0.2 reshape.96
  141.4 27.8 %all_to_all.5 = bf16[128,2,512]{2,1,0:T(2,128)(2,1)S(1)} all-to-all(bf16[128,2,512]{2,1,0:T(2,128)(2,1)S(1)} %reshape.96), channel_id=1, replica_groups=mesh['req'=128,'tp'=2] {'req'}, dimensions={0} | all-to-all | bytes 524288 | tf_op jit(solution)/shard_map/all_to_all | solution.py:114
  169.3 0.2 reshape.97
  169.5 0.3 convolution_reduce_fusion
  169.8 72.4 %pmax.7 = f32[128]{0:T(128)S(1)} all-reduce(f32[128]{0:T(128)S(1)} %convolution_reduce_fusion), channel_id=1, replica_groups=mesh['req'=128,'tp'=2] {'req','tp'}, use_global_device_ids=true, to_apply=%region_13.14 | all-reduce | flops 128 | bytes 1024 | tf_op jit(solution)/shard_map/pmax | solution.py:120
  242.2 0.6 dynamic_slice.21
  (57 shorter events, 0.5 us)
Async XLA Ops:
  7.2 86.9 %copy-start = (bf16[1024,1024]{1,0:T(8,128)(2,1)S(1)}, bf16[1024,1024]{1,0:T(8,128)(2,1)}, u32[]{:S(2)}) copy-start(bf16[1024,1024]{1,0:T(8,128)(2,1)} %param.26) | copy-start | bytes 6291460
  7.2 5.4 %copy-start.3 = (bf16[512,1024]{1,0:T(8,128)(2,1)S(1)}, bf16[512,1024]{1,0:T(8,128)(2,1)}, u32[]{:S(2)}) copy-start(bf16[512,1024]{1,0:T(8,128)(2,1)} %param.16) | copy-start | bytes 3145732
  7.2 84.0 %all-reduce.3.cloned.1.call-start = ((), (), s32[]{:S(2)}) async-start(), calls=%async_computation.1 | async-start | bytes 2097152 | tf_op jit(solution)/shard_map/psum | solution.py:95
  9.4 3.2 %copy-start.12 = (bf16[1024,512]{1,0:T(8,128)(2,1)S(1)}, bf16[1024,512]{1,0:T(8,128)(2,1)}, u32[]{:S(2)}) copy-start(bf16[1024,512]{1,0:T(8,128)(2,1)} %param.21) | copy-start | bytes 3145732
  13.4 1.5 copy-start.2
  14.9 3.2 %copy-start.1 = (f32[8,512,512]{2,1,0:T(8,128)}, f32[8,512,512]{2,1,0:T(8,128)S(1)}, u32[]{:S(2)}) copy-start(f32[8,512,512]{2,1,0:T(8,128)S(1)} %get-tuple-element.83) | copy-start | bytes 25165828
  14.9 3.2 %copy-start.13 = (bf16[1024,512]{1,0:T(8,128)(2,1)S(1)}, bf16[1024,512]{1,0:T(8,128)(2,1)}, u32[]{:S(2)}) copy-start(bf16[1024,512]{1,0:T(8,128)(2,1)} %param.23) | copy-start | bytes 3145732
  19.7 2.4 copy-start.9
  53.3 3.1 %copy-start.10 = (f32[2,1024]{1,0:T(2,128)S(1)}, f32[2,1024]{1,0:T(2,128)}, u32[]{:S(2)}) copy-start(f32[2,1024]{1,0:T(2,128)} %param.28) | copy-start | bytes 24580
  53.3 3.1 %copy-start.11 = (f32[2,1024]{1,0:T(2,128)S(1)}, f32[2,1024]{1,0:T(2,128)}, u32[]{:S(2)}) copy-start(f32[2,1024]{1,0:T(2,128)} %param.27) | copy-start | bytes 24580
  53.3 37.9 %copy-start.4 = (bf16[512,1024]{1,0:T(8,128)(2,1)S(1)}, bf16[512,1024]{1,0:T(8,128)(2,1)}, u32[]{:S(2)}) copy-start(bf16[512,1024]{1,0:T(8,128)(2,1)} %param.16) | copy-start | bytes 3145732
  56.3 78.2 %all-reduce.5.cloned.1.call-start = ((), (), s32[]{:S(2)}) async-start(), calls=%async_computation.2 | async-start | bytes 2097152 | tf_op jit(solution)/shard_map/psum | solution.py:104
  91.2 1.7 copy-start.7
  91.2 2.2 copy-start.5
  134.6 1.7 copy-start.6
  137.3 1.0 copy-start.8
  138.3 31.2 %copy-start.14 = (bf16[192,1024]{1,0:T(8,128)(2,1)S(1)}, bf16[192,1024]{1,0:T(8,128)(2,1)}, u32[]{:S(2)}) copy-start(bf16[192,1024]{1,0:T(8,128)(2,1)} %param.29) | copy-start | bytes 1179652
  169.8 73.0 %copy-start.15 = (f32[128]{0:T(128)}, f32[128]{0:T(128)S(1)}, u32[]{:S(2)}) copy-start(f32[128]{0:T(128)S(1)} %convolution_reduce_fusion) | copy-start | bytes 1540
Sparse Core Ops, SparseCore 0:
  56.5 34.7 all-reduce.2
  103.0 31.5 all-reduce.4
